TPU v7x, 256 devices: a whole 4x4x8 slice. The times are simulated.
256 devices in a mesh: row: 16 (over y, x), col: 16 (over z, core).
Axes of the slice: x: 4, y: 4, z: 8, core: 2. Of those that a mesh axis runs over, the one named last changes fastest.
Arguments:
- q_seq: bfloat16 [2048, 6144], P('row', 'col'), may hold values from -4.5 to 4.5
- k_seq: bfloat16 [2048, 6144], P('row', 'col'), may hold values from -4.5 to 4.5
- v_seq: bfloat16 [2048, 6144], P('row', 'col'), may hold values from -6 to 6
- resid: bfloat16 [2048, 6144], P('row', 'col'), may hold values from -90 to 90
- ln_gain: float32 [6144], replicated, may hold values from 0.1 to 1.9
- w_up: bfloat16 [6144, 24576], P('row', 'col'), may hold values from -0.078125 to 0.078125
Outputs:
- hidden: bfloat16 [2048, 24576], P('row', 'col')
All inputs are finite; a program needn't handle non-finite values.
Results may differ from a plain program's by a relative error of at most 0.0051.
Values may be sent and summed in bfloat16 or wider, within the bound.
No kernel may reach another device: no remote copies, remote signals or barrier semaphores. Data moves between devices by JAX's collectives and lax.ppermute only.
A program may use at most 64 MiB of HBM per device.

v0:
```python
import math
import jax
import jax.numpy as jnp
from jax import lax
from jax.sharding import PartitionSpec as P

HD = 128


def attention_block(query, keys, values):
    seq, width = query.shape
    heads = width // HD
    qshaped = query.reshape(seq, heads, HD)
    kshaped = keys.reshape(seq, heads, HD)
    vshaped = values.reshape(seq, heads, HD)
    scores = jnp.einsum("qhd,khd->hqk", qshaped, kshaped, preferred_element_type=jnp.float32)
    scores = scores * (1.0 / math.sqrt(HD))
    rows_idx = lax.broadcasted_iota(jnp.int32, (seq, seq), 0)
    cols_idx = lax.broadcasted_iota(jnp.int32, (seq, seq), 1)
    scores = jnp.where((rows_idx >= cols_idx)[None], scores, -1e30)
    highest = jnp.max(scores, axis=-1, keepdims=True)
    expo = jnp.exp(scores - highest)
    prob = (expo / jnp.sum(expo, axis=-1, keepdims=True)).astype(jnp.bfloat16)
    output = jnp.einsum("hqk,khd->qhd", prob, vshaped, preferred_element_type=jnp.float32)
    return output.astype(jnp.bfloat16).reshape(seq, width)


def scale_rows(stream, mean, spread, gain):
    return ((stream - mean) * lax.rsqrt(spread + 1e-05) * gain[None, :]).astype(jnp.bfloat16)


def per_device(q_seq, k_seq, v_seq, resid, ln_gain, w_up):
    attended = attention_block(q_seq, k_seq, v_seq)
    returned, res_tokens = (
        lax.all_to_all(attended, "col", split_axis=0, concat_axis=1, tiled=True),
        lax.all_to_all(resid, "col", split_axis=0, concat_axis=1, tiled=True),
    )
    stream = res_tokens.astype(jnp.float32) + returned.astype(jnp.float32)
    full_width = stream.shape[1]
    mean = jnp.sum(stream, axis=1, keepdims=True) / full_width
    spread = jnp.sum(stream * stream, axis=1, keepdims=True) / full_width - mean * mean
    normed_tokens = scale_rows(stream, mean, spread, ln_gain)
    normed = lax.all_to_all(normed_tokens, "col", split_axis=1, concat_axis=0, tiled=True)
    whole = lax.all_gather(normed, "col", axis=1, tiled=True)
    product = jnp.dot(
        whole, lax.all_gather(w_up, "row", axis=0, tiled=True), preferred_element_type=jnp.float32
    )
    return jax.nn.gelu(product, approximate=True).astype(jnp.bfloat16)


def solution(mesh):
    placed = (
        P("row", "col"),
        P("row", "col"),
        P("row", "col"),
        P("row", "col"),
        P(),
        P("row", "col"),
    )
    return jax.shard_map(
        per_device, mesh=mesh, in_specs=placed, out_specs=P("row", "col"), check_vma=False
    )
```

profile of v0, /device:TPU:1, one launch (start us, length us, event | category | flops | bytes accessed | tf_op | source)
XLA Modules:
  0.0 229.7 jit_solution(653046495785371151)
XLA Ops:
  6.5 0.0 copy-start
  6.5 10.1 %all-to-all-start = ((bf16[16,8,384]{2,1,0:T(8,128)(2,1)}), bf16[16,8,384]{2,1,0:T(8,128)(2,1)S(1)}, u32[]{:S(2)}, u32[]{:S(2)}) async-start(bf16[16,8,384]{2,1,0:T(8,128)(2,1)} %bitcast.21), calls=%async_computation | async-start | bytes 196608 | tf_op jit(solution)/shard_map/all_to_all | solution.py:36
  16.7 1.0 copy.11
  17.7 1.0 copy.12
  18.7 0.2 fusion.2
  18.9 0.1 fusion.17
  19.0 1.0 copy.15
  20.0 0.3 fusion.4
  20.3 0.1 copy.18
  20.4 0.7 all_to_all.34
  21.1 4.0 %all-to-all-done = bf16[16,8,384]{2,1,0:T(8,128)(2,1)S(1)} async-done(((bf16[16,8,384]{2,1,0:T(8,128)(2,1)}), bf16[16,8,384]{2,1,0:T(8,128)(2,1)S(1)}, u32[]{:S(2)}, u32[]{:S(2)}) %all-to-all-start) | async-done | bytes 98336 | tf_op jit(solution)/shard_map/all_to_all | solution.py:36
  25.1 3.4 %all-to-all-start.1 = ((bf16[16,8,384]{2,1,0:T(8,128)(2,1)}), bf16[16,8,384]{2,1,0:T(8,128)(2,1)S(1)}, u32[]{:S(2)}, u32[]{:S(2)}) async-start(bf16[16,8,384]{2,1,0:T(8,128)(2,1)} %all_to_all.34), calls=%async_computation.1 | async-start | bytes 196608 | tf_op jit(solution)/shard_map/all_to_all | solution.py:35
  28.6 0.0 all-gather.3.cloned.1.call-start
  28.6 0.0 copy-done
  28.6 8.3 %all-to-all-done.1 = bf16[16,8,384]{2,1,0:T(8,128)(2,1)S(1)} async-done(((bf16[16,8,384]{2,1,0:T(8,128)(2,1)}), bf16[16,8,384]{2,1,0:T(8,128)(2,1)S(1)}, u32[]{:S(2)}, u32[]{:S(2)}) %all-to-all-start.1) | async-done | bytes 98336 | tf_op jit(solution)/shard_map/all_to_all | solution.py:35
  36.9 0.2 fusion.13
  37.1 0.1 fusion.14
  37.2 11.6 %all_to_all.42 = bf16[8,16,384]{2,0,1:T(8,128)(2,1)} all-to-all(bf16[8,16,384]{2,0,1:T(8,128)(2,1)S(1)} %fusion.14), channel_id=1, replica_groups=mesh['row'=16,'col'=16] {'col'}, dimensions={1} | all-to-all | bytes 196608 | tf_op jit(solution)/shard_map/all_to_all | solution.py:43
  48.8 0.0 all-gather.3.cloned.1.call-update
  48.8 0.0 all-gather.5.cloned.1.call-start
  48.9 0.7 all-gather.5.cloned.1.call-update
  49.6 35.2 %all-gather.3.cloned.1.call-done = bf16[128,6144]{1,0:T(8,128)(2,1)} async-done(((bf16[128,384]{1,0:T(8,128)(2,1)}), bf16[128,6144]{1,0:T(8,128)(2,1)}) %all-gather.3.cloned.1.call-update) | async-done | bytes 1572880 | tf_op jit(solution)/shard_map/all_gather | solution.py:44
  84.8 127.7 %all-gather.5.cloned.1.call-done = bf16[6144,1536]{1,0:T(8,128)(2,1)} async-done(((bf16[384,1536]{1,0:T(8,128)(2,1)}), bf16[6144,1536]{1,0:T(8,128)(2,1)}) %all-gather.5.cloned.1.call-update) | async-done | bytes 18874384 | tf_op jit(solution)/shard_map/all_gather | solution.py:46
  212.5 10.4 %fusion.12 = bf16[128,1536]{1,0:T(8,128)(2,1)} fusion(bf16[128,6144]{1,0:T(8,128)(2,1)} %all-gather.3.cloned.1.call-done, bf16[6144,1536]{1,0:T(8,128)(2,1)} %all-gather.5.cloned.1.call-done), kind=kOutput, calls=%fused_computation.15 | convolution fusion | flops 2417688576 | bytes 20840448 | tf_op jit(solution)/shard_map/dot_general | solution.py:45
  (3 shorter events, 0.0 us)
Async XLA Ops:
  6.5 22.1 %copy-start = (f32[6144]{0:T(1024)S(1)}, f32[6144]{0:T(1024)}, u32[]{:S(2)}) copy-start(f32[6144]{0:T(1024)} %param.10) | copy-start | bytes 73732
  6.5 18.6 %all-to-all-start = ((bf16[16,8,384]{2,1,0:T(8,128)(2,1)}), bf16[16,8,384]{2,1,0:T(8,128)(2,1)S(1)}, u32[]{:S(2)}, u32[]{:S(2)}) async-start(bf16[16,8,384]{2,1,0:T(8,128)(2,1)} %bitcast.21), calls=%async_computation | async-start | bytes 196608 | tf_op jit(solution)/shard_map/all_to_all | solution.py:36
  25.1 11.8 %all-to-all-start.1 = ((bf16[16,8,384]{2,1,0:T(8,128)(2,1)}), bf16[16,8,384]{2,1,0:T(8,128)(2,1)S(1)}, u32[]{:S(2)}, u32[]{:S(2)}) async-start(bf16[16,8,384]{2,1,0:T(8,128)(2,1)} %all_to_all.34), calls=%async_computation.1 | async-start | bytes 196608 | tf_op jit(solution)/shard_map/all_to_all | solution.py:35
  28.6 56.2 %all-gather.3.cloned.1.call-start = ((), (), s32[]{:S(2)}) async-start(), calls=%async_computation.3 | async-start | bytes 1671168 | tf_op jit(solution)/shard_map/all_gather | solution.py:44
  48.8 163.7 %all-gather.5.cloned.1.call-start = ((), (), s32[]{:S(2)}) async-start(), calls=%async_computation.4 | async-start | bytes 20054016 | tf_op jit(solution)/shard_map/all_gather | solution.py:46
Sparse Core Ops, SparseCore 0:
  48.9 35.7 all-gather.2
  87.2 125.2 all-gather.4
where the time goes:
time: 230 us
  waiting for transfers between devices  176 us (77%)
  starting transfers between devices  13.6 us (6%)
  between operations  13.5 us (6%)
  blocking collectives  11.6 us (5%)
  matrix products  10.9 us (5%)
  local copies, waits for them, and re-layouts  3.85 us (2%)
    all_gather x1, waiting for transfers between devices, per_device(): lax.all_gather(w_up, 'row', axis=0, tiled=True)  128 us
    all_gather x1, waiting for transfers between devices, per_device(): whole = lax.all_gather(normed, 'col', axis=1, tiled=True)  35.2 us
    all_to_all x1, blocking collectives, per_device(): lax.all_to_all(normed_tokens, 'col', split_axis=1, concat_axis=0, tiled=T...  11.6 us
    dot_general x1, matrix products, per_device(): jnp.dot(whole, lax.all_gather(w_up, 'row', axis=0, tiled=True), preferred...  10.4 us
    all_to_all x1, starting transfers between devices, per_device(): lax.all_to_all(resid, 'col', split_axis=0, concat_axis=1, tiled=True)  10.1 us
    all_to_all x1, waiting for transfers between devices, per_device(): lax.all_to_all(attended, 'col', split_axis=0, concat_axis=1, tiled=True)  8.27 us
  transfers between devices with their start and end apart: 4, of which 4 were waited for; matrix products, arithmetic and copies ran while one was open for 2% of the time, Pallas kernels for 0%

commit v1 on v0

--- a/solution.py
+++ b/solution.py
@@ -41,7 +41,12 @@
     spread = jnp.sum(stream * stream, axis=1, keepdims=True) / full_width - mean * mean
     normed_tokens = scale_rows(stream, mean, spread, ln_gain)
     normed = lax.all_to_all(normed_tokens, "col", split_axis=1, concat_axis=0, tiled=True)
-    whole = lax.all_gather(normed, "col", axis=1, tiled=True)
+    ring = [normed]
+    for hop in range(15):
+        ring.append(lax.ppermute(ring[-1], "col", [(dev, (dev + 1) % 16) for dev in range(16)]))
+    whole = jnp.roll(
+        jnp.concatenate(ring[::-1], axis=1), (lax.axis_index("col") + 1) * ring[0].shape[1], axis=1
+    )
     product = jnp.dot(
         whole, lax.all_gather(w_up, "row", axis=0, tiled=True), preferred_element_type=jnp.float32
     )

time: 230 us -> 166 us (0.72)
  the two profiles are of different devices: /device:TPU:1 before, /device:TPU:14 now
where the time goes in v1:
time: 166 us
  waiting for transfers between devices  86.6 us (52%)
  blocking collectives  27.5 us (17%)
  local copies, waits for them, and re-layouts  22.5 us (14%)
  between operations  13.8 us (8%)
  matrix products  10.6 us (6%)
  starting transfers between devices  4.12 us (2%)
    ppermute x15, waiting for transfers between devices, per_device(): lax.ppermute(ring[-1], 'col', [(dev, (dev + 1) % 16) for dev in range(16)])  77.6 us
    unnamed x80, local copies, waits for them, and re-layouts  22.3 us
    all_to_all x1, blocking collectives, per_device(): lax.all_to_all(attended, 'col', split_axis=0, concat_axis=1, tiled=True)  16.7 us
    all_to_all x1, blocking collectives, per_device(): lax.all_to_all(normed_tokens, 'col', split_axis=1, concat_axis=0, tiled=T...  10.9 us
    dot_general x1, matrix products, per_device(): jnp.dot(whole, lax.all_gather(w_up, 'row', axis=0, tiled=True), preferred...  10.1 us
    all_to_all x1, waiting for transfers between devices, per_device(): lax.all_to_all(resid, 'col', split_axis=0, concat_axis=1, tiled=True)  8.25 us
    all_to_all x1, starting transfers between devices, per_device(): lax.all_to_all(resid, 'col', split_axis=0, concat_axis=1, tiled=True)  3.51 us
  transfers between devices with their start and end apart: 17, of which 16 were waited for; matrix products, arithmetic and copies ran while one was open for 10% of the time, Pallas kernels for 0%

profile of v1, /device:TPU:14, one launch (start us, length us, event | category | flops | bytes accessed | tf_op | source)
XLA Modules:
  0.0 165.5 jit_solution(12327807186033235035)
XLA Ops:
  6.5 0.7 all-gather.2.cloned.1.call-update
  7.3 1.0 copy.11
  8.3 1.0 copy.12
  9.3 1.0 copy.15
  10.3 0.2 fusion.4
  10.6 0.1 fusion.24
  10.6 0.3 fusion.6
  10.9 0.1 copy.18
  11.0 0.1 all_to_all.34
  11.1 16.7 %all_to_all.42 = bf16[16,8,384]{2,1,0:T(8,128)(2,1)S(1)} all-to-all(bf16[16,8,384]{2,1,0:T(8,128)(2,1)S(1)} %all_to_all.34), channel_id=1, replica_groups=mesh['row'=16,'col'=16] {'col'}, dimensions={0} | all-to-all | bytes 196608 | tf_op jit(solution)/shard_map/all_to_all | solution.py:35
  27.8 3.5 %all-to-all-start = ((bf16[16,8,384]{2,1,0:T(8,128)(2,1)}), bf16[16,8,384]{2,1,0:T(8,128)(2,1)S(1)}, u32[]{:S(2)}, u32[]{:S(2)}) async-start(bf16[16,8,384]{2,1,0:T(8,128)(2,1)} %bitcast), calls=%async_computation | async-start | bytes 196608 | tf_op jit(solution)/shard_map/all_to_all | solution.py:36
  31.3 8.3 %all-to-all-done = bf16[16,8,384]{2,1,0:T(8,128)(2,1)S(1)} async-done(((bf16[16,8,384]{2,1,0:T(8,128)(2,1)}), bf16[16,8,384]{2,1,0:T(8,128)(2,1)S(1)}, u32[]{:S(2)}, u32[]{:S(2)}) %all-to-all-start) | async-done | bytes 98336 | tf_op jit(solution)/shard_map/all_to_all | solution.py:36
  39.6 0.2 fusion.19
  39.8 0.1 fusion.20
  39.9 10.9 %all_to_all.43 = bf16[8,16,384]{2,0,1:T(8,128)(2,1)S(1)} all-to-all(bf16[8,16,384]{2,0,1:T(8,128)(2,1)S(1)} %fusion.20), channel_id=1, replica_groups=mesh['row'=16,'col'=16] {'col'}, dimensions={1} | all-to-all | bytes 196608 | tf_op jit(solution)/shard_map/all_to_all | solution.py:43
  50.7 0.6 collective-permute-start
  51.3 4.7 %collective-permute-done = bf16[128,384]{1,0:T(8,128)(2,1)S(1)} collective-permute-done((bf16[128,384]{1,0:T(8,128)(2,1)S(1)}, bf16[128,384]{1,0:T(8,128)(2,1)S(1)}, u32[]{:S(2)}, u32[]{:S(2)}) %collective-permute-start) | collective-permute-done | bytes 98336 | tf_op jit(solution)/shard_map/ppermute | solution.py:46
  56.0 0.0 collective-permute-start.1
  56.0 5.2 %collective-permute-done.1 = bf16[128,384]{1,0:T(8,128)(2,1)S(1)} collective-permute-done((bf16[128,384]{1,0:T(8,128)(2,1)S(1)}, bf16[128,384]{1,0:T(8,128)(2,1)S(1)}, u32[]{:S(2)}, u32[]{:S(2)}) %collective-permute-start.1) | collective-permute-done | bytes 98336 | tf_op jit(solution)/shard_map/ppermute | solution.py:46
  61.2 0.0 collective-permute-start.2
  61.3 5.2 %collective-permute-done.2 = bf16[128,384]{1,0:T(8,128)(2,1)S(1)} collective-permute-done((bf16[128,384]{1,0:T(8,128)(2,1)S(1)}, bf16[128,384]{1,0:T(8,128)(2,1)S(1)}, u32[]{:S(2)}, u32[]{:S(2)}) %collective-permute-start.2) | collective-permute-done | bytes 98336 | tf_op jit(solution)/shard_map/ppermute | solution.py:46
  66.5 0.0 collective-permute-start.3
  66.5 5.2 %collective-permute-done.3 = bf16[128,384]{1,0:T(8,128)(2,1)S(1)} collective-permute-done((bf16[128,384]{1,0:T(8,128)(2,1)S(1)}, bf16[128,384]{1,0:T(8,128)(2,1)S(1)}, u32[]{:S(2)}, u32[]{:S(2)}) %collective-permute-start.3) | collective-permute-done | bytes 98336 | tf_op jit(solution)/shard_map/ppermute | solution.py:46
  71.8 0.6 copy-done
  72.4 0.0 collective-permute-start.4
  72.4 5.2 %collective-permute-done.4 = bf16[128,384]{1,0:T(8,128)(2,1)S(1)} collective-permute-done((bf16[128,384]{1,0:T(8,128)(2,1)S(1)}, bf16[128,384]{1,0:T(8,128)(2,1)S(1)}, u32[]{:S(2)}, u32[]{:S(2)}) %collective-permute-start.4) | collective-permute-done | bytes 98336 | tf_op jit(solution)/shard_map/ppermute | solution.py:46
  77.6 0.6 copy-done.2
  78.3 0.0 collective-permute-start.5
  78.3 5.2 %collective-permute-done.5 = bf16[128,384]{1,0:T(8,128)(2,1)S(1)} collective-permute-done((bf16[128,384]{1,0:T(8,128)(2,1)S(1)}, bf16[128,384]{1,0:T(8,128)(2,1)S(1)}, u32[]{:S(2)}, u32[]{:S(2)}) %collective-permute-start.5) | collective-permute-done | bytes 98336 | tf_op jit(solution)/shard_map/ppermute | solution.py:46
  83.5 0.6 copy-done.4
  84.2 5.2 %collective-permute-done.6 = bf16[128,384]{1,0:T(8,128)(2,1)S(1)} collective-permute-done((bf16[128,384]{1,0:T(8,128)(2,1)S(1)}, bf16[128,384]{1,0:T(8,128)(2,1)S(1)}, u32[]{:S(2)}, u32[]{:S(2)}) %collective-permute-start.6) | collective-permute-done | bytes 98336 | tf_op jit(solution)/shard_map/ppermute | solution.py:46
  89.4 0.6 copy-done.6
  90.1 5.2 %collective-permute-done.7 = bf16[128,384]{1,0:T(8,128)(2,1)S(1)} collective-permute-done((bf16[128,384]{1,0:T(8,128)(2,1)S(1)}, bf16[128,384]{1,0:T(8,128)(2,1)S(1)}, u32[]{:S(2)}, u32[]{:S(2)}) %collective-permute-start.7) | collective-permute-done | bytes 98336 | tf_op jit(solution)/shard_map/ppermute | solution.py:46
  95.3 0.6 copy-done.8
  95.9 0.0 collective-permute-start.8
  96.0 5.2 %collective-permute-done.8 = bf16[128,384]{1,0:T(8,128)(2,1)S(1)} collective-permute-done((bf16[128,384]{1,0:T(8,128)(2,1)S(1)}, bf16[128,384]{1,0:T(8,128)(2,1)S(1)}, u32[]{:S(2)}, u32[]{:S(2)}) %collective-permute-start.8) | collective-permute-done | bytes 98336 | tf_op jit(solution)/shard_map/ppermute | solution.py:46
  101.2 0.6 copy-done.10
  101.8 0.0 collective-permute-start.9
  101.9 5.2 %collective-permute-done.9 = bf16[128,384]{1,0:T(8,128)(2,1)S(1)} collective-permute-done((bf16[128,384]{1,0:T(8,128)(2,1)S(1)}, bf16[128,384]{1,0:T(8,128)(2,1)S(1)}, u32[]{:S(2)}, u32[]{:S(2)}) %collective-permute-start.9) | collective-permute-done | bytes 98336 | tf_op jit(solution)/shard_map/ppermute | solution.py:46
  107.1 0.6 copy-done.12
  107.7 5.2 %collective-permute-done.10 = bf16[128,384]{1,0:T(8,128)(2,1)S(1)} collective-permute-done((bf16[128,384]{1,0:T(8,128)(2,1)S(1)}, bf16[128,384]{1,0:T(8,128)(2,1)S(1)}, u32[]{:S(2)}, u32[]{:S(2)}) %collective-permute-start.10) | collective-permute-done | bytes 98336 | tf_op jit(solution)/shard_map/ppermute | solution.py:46
  113.0 0.6 copy-done.14
  113.6 5.2 %collective-permute-done.11 = bf16[128,384]{1,0:T(8,128)(2,1)S(1)} collective-permute-done((bf16[128,384]{1,0:T(8,128)(2,1)S(1)}, bf16[128,384]{1,0:T(8,128)(2,1)S(1)}, u32[]{:S(2)}, u32[]{:S(2)}) %collective-permute-start.11) | collective-permute-done | bytes 98336 | tf_op jit(solution)/shard_map/ppermute | solution.py:46
  118.9 0.6 copy-done.16
  119.5 5.2 %collective-permute-done.12 = bf16[128,384]{1,0:T(8,128)(2,1)S(1)} collective-permute-done((bf16[128,384]{1,0:T(8,128)(2,1)S(1)}, bf16[128,384]{1,0:T(8,128)(2,1)S(1)}, u32[]{:S(2)}, u32[]{:S(2)}) %collective-permute-start.12) | collective-permute-done | bytes 98336 | tf_op jit(solution)/shard_map/ppermute | solution.py:46
  124.8 0.6 copy-done.18
  125.4 5.2 %collective-permute-done.13 = bf16[128,384]{1,0:T(8,128)(2,1)S(1)} collective-permute-done((bf16[128,384]{1,0:T(8,128)(2,1)S(1)}, bf16[128,384]{1,0:T(8,128)(2,1)S(1)}, u32[]{:S(2)}, u32[]{:S(2)}) %collective-permute-start.13) | collective-permute-done | bytes 98336 | tf_op jit(solution)/shard_map/ppermute | solution.py:46
  130.7 0.6 copy-done.20
  131.4 4.6 %collective-permute-done.14 = bf16[128,384]{1,0:T(8,128)(2,1)} collective-permute-done((bf16[128,384]{1,0:T(8,128)(2,1)S(1)}, bf16[128,384]{1,0:T(8,128)(2,1)}, u32[]{:S(2)}, u32[]{:S(2)}) %collective-permute-start.14) | collective-permute-done | bytes 98336 | tf_op jit(solution)/shard_map/ppermute | solution.py:46
  136.0 0.9 constant_dynamic-update-slice_fusion.31
  137.0 0.9 constant_dynamic-update-slice_fusion.30
  137.9 0.9 constant_dynamic-update-slice_fusion.29
  138.8 0.9 constant_dynamic-update-slice_fusion.28
  139.7 0.9 constant_dynamic-update-slice_fusion.27
  140.6 0.9 constant_dynamic-update-slice_fusion.26
  141.6 0.9 constant_dynamic-update-slice_fusion.25
  142.5 0.9 constant_dynamic-update-slice_fusion.24
  143.4 0.9 constant_dynamic-update-slice_fusion.23
  144.3 0.9 constant_dynamic-update-slice_fusion.22
  145.2 0.9 constant_dynamic-update-slice_fusion.21
  146.1 0.9 constant_dynamic-update-slice_fusion.20
  147.2 0.9 constant_dynamic-update-slice_fusion.15
  148.6 0.0 all-gather.2.cloned.1.call-done
  148.6 10.1 %fusion.16 = bf16[128,1536]{1,0:T(8,128)(2,1)} fusion(bf16[6144,1536]{1,0:T(8,128)(2,1)} %all-gather.2.cloned.1.call-done, bf16[128,12288]{1,0:T(8,128)(2,1)S(1)} %constant_dynamic-update-slice_fusion, s32[]{:T(128)S(6)} %select_n.19), kind=kOutput, calls=%fused_computation.17 | convolution fusion | flops 2417688576 | bytes 20840452 | tf_op jit(solution)/shard_map/dot_general | solution.py:50
  (65 shorter events, 0.5 us)
Async XLA Ops:
  6.5 24.8 %copy-start.22 = (f32[6144]{0:T(1024)S(1)}, f32[6144]{0:T(1024)}, u32[]{:S(2)}) copy-start(f32[6144]{0:T(1024)} %param.10) | copy-start | bytes 73732
  6.5 142.1 %all-gather.2.cloned.1.call-start = ((), (), s32[]{:S(2)}) async-start(), calls=%async_computation.3 | async-start | bytes 20054016 | tf_op jit(solution)/shard_map/all_gather | solution.py:51
  27.8 11.8 %all-to-all-start = ((bf16[16,8,384]{2,1,0:T(8,128)(2,1)}), bf16[16,8,384]{2,1,0:T(8,128)(2,1)S(1)}, u32[]{:S(2)}, u32[]{:S(2)}) async-start(bf16[16,8,384]{2,1,0:T(8,128)(2,1)} %bitcast), calls=%async_computation | async-start | bytes 196608 | tf_op jit(solution)/shard_map/all_to_all | solution.py:36
  50.7 5.3 %collective-permute-start = (bf16[128,384]{1,0:T(8,128)(2,1)S(1)}, bf16[128,384]{1,0:T(8,128)(2,1)S(1)}, u32[]{:S(2)}, u32[]{:S(2)}) collective-permute-start(bf16[128,384]{1,0:T(8,128)(2,1)S(1)} %bitcast.19), channel_id=1, source_target_pairs={{0,1},{1,2},{2,3},{3,4},{4,5},{5,6},{6,7},{7,8},{8,9},{9,10},{10,1... | collective-permute-start | bytes 294920 | tf_op jit(solution)/shard_map/ppermute | solution.py:46
  56.0 5.3 %collective-permute-start.1 = (bf16[128,384]{1,0:T(8,128)(2,1)S(1)}, bf16[128,384]{1,0:T(8,128)(2,1)S(1)}, u32[]{:S(2)}, u32[]{:S(2)}) collective-permute-start(bf16[128,384]{1,0:T(8,128)(2,1)S(1)} %collective-permute-done), channel_id=1, source_target_pairs={{0,1},{1,2},{2,3},{3,4},{4,5},{5,6},{6,7},{7,8},{8,9},{9,10},{10,1... | collective-permute-start | bytes 294920 | tf_op jit(solution)/shard_map/ppermute | solution.py:46
  61.2 5.3 %collective-permute-start.2 = (bf16[128,384]{1,0:T(8,128)(2,1)S(1)}, bf16[128,384]{1,0:T(8,128)(2,1)S(1)}, u32[]{:S(2)}, u32[]{:S(2)}) collective-permute-start(bf16[128,384]{1,0:T(8,128)(2,1)S(1)} %collective-permute-done.1), channel_id=1, source_target_pairs={{0,1},{1,2},{2,3},{3,4},{4,5},{5,6},{6,7},{7,8},{8,9},{9,10},{10,1... | collective-permute-start | bytes 294920 | tf_op jit(solution)/shard_map/ppermute | solution.py:46
  66.5 5.3 %collective-permute-start.3 = (bf16[128,384]{1,0:T(8,128)(2,1)S(1)}, bf16[128,384]{1,0:T(8,128)(2,1)S(1)}, u32[]{:S(2)}, u32[]{:S(2)}) collective-permute-start(bf16[128,384]{1,0:T(8,128)(2,1)S(1)} %collective-permute-done.2), channel_id=1, source_target_pairs={{0,1},{1,2},{2,3},{3,4},{4,5},{5,6},{6,7},{7,8},{8,9},{9,10},{10,1... | collective-permute-start | bytes 294920 | tf_op jit(solution)/shard_map/ppermute | solution.py:46
  71.8 0.6 copy-start
  72.4 5.3 %collective-permute-start.4 = (bf16[128,384]{1,0:T(8,128)(2,1)S(1)}, bf16[128,384]{1,0:T(8,128)(2,1)S(1)}, u32[]{:S(2)}, u32[]{:S(2)}) collective-permute-start(bf16[128,384]{1,0:T(8,128)(2,1)S(1)} %collective-permute-done.3), channel_id=1, source_target_pairs={{0,1},{1,2},{2,3},{3,4},{4,5},{5,6},{6,7},{7,8},{8,9},{9,10},{10,1... | collective-permute-start | bytes 294920 | tf_op jit(solution)/shard_map/ppermute | solution.py:46
  77.6 0.6 copy-start.2
  78.3 5.3 %collective-permute-start.5 = (bf16[128,384]{1,0:T(8,128)(2,1)S(1)}, bf16[128,384]{1,0:T(8,128)(2,1)S(1)}, u32[]{:S(2)}, u32[]{:S(2)}) collective-permute-start(bf16[128,384]{1,0:T(8,128)(2,1)S(1)} %collective-permute-done.4), channel_id=1, source_target_pairs={{0,1},{1,2},{2,3},{3,4},{4,5},{5,6},{6,7},{7,8},{8,9},{9,10},{10,1... | collective-permute-start | bytes 294920 | tf_op jit(solution)/shard_map/ppermute | solution.py:46
  83.5 0.6 copy-start.4
  84.2 5.3 %collective-permute-start.6 = (bf16[128,384]{1,0:T(8,128)(2,1)S(1)}, bf16[128,384]{1,0:T(8,128)(2,1)S(1)}, u32[]{:S(2)}, u32[]{:S(2)}) collective-permute-start(bf16[128,384]{1,0:T(8,128)(2,1)S(1)} %collective-permute-done.5), channel_id=1, source_target_pairs={{0,1},{1,2},{2,3},{3,4},{4,5},{5,6},{6,7},{7,8},{8,9},{9,10},{10,1... | collective-permute-start | bytes 294920 | tf_op jit(solution)/shard_map/ppermute | solution.py:46
  89.4 0.6 copy-start.6
  90.1 5.3 %collective-permute-start.7 = (bf16[128,384]{1,0:T(8,128)(2,1)S(1)}, bf16[128,384]{1,0:T(8,128)(2,1)S(1)}, u32[]{:S(2)}, u32[]{:S(2)}) collective-permute-start(bf16[128,384]{1,0:T(8,128)(2,1)S(1)} %collective-permute-done.6), channel_id=1, source_target_pairs={{0,1},{1,2},{2,3},{3,4},{4,5},{5,6},{6,7},{7,8},{8,9},{9,10},{10,1... | collective-permute-start | bytes 294920 | tf_op jit(solution)/shard_map/ppermute | solution.py:46
  95.3 0.6 copy-start.8
  95.9 5.3 %collective-permute-start.8 = (bf16[128,384]{1,0:T(8,128)(2,1)S(1)}, bf16[128,384]{1,0:T(8,128)(2,1)S(1)}, u32[]{:S(2)}, u32[]{:S(2)}) collective-permute-start(bf16[128,384]{1,0:T(8,128)(2,1)S(1)} %collective-permute-done.7), channel_id=1, source_target_pairs={{0,1},{1,2},{2,3},{3,4},{4,5},{5,6},{6,7},{7,8},{8,9},{9,10},{10,1... | collective-permute-start | bytes 294920 | tf_op jit(solution)/shard_map/ppermute | solution.py:46
  101.2 0.6 copy-start.10
  101.8 5.3 %collective-permute-start.9 = (bf16[128,384]{1,0:T(8,128)(2,1)S(1)}, bf16[128,384]{1,0:T(8,128)(2,1)S(1)}, u32[]{:S(2)}, u32[]{:S(2)}) collective-permute-start(bf16[128,384]{1,0:T(8,128)(2,1)S(1)} %collective-permute-done.8), channel_id=1, source_target_pairs={{0,1},{1,2},{2,3},{3,4},{4,5},{5,6},{6,7},{7,8},{8,9},{9,10},{10,1... | collective-permute-start | bytes 294920 | tf_op jit(solution)/shard_map/ppermute | solution.py:46
  107.1 0.6 copy-start.12
  107.7 5.3 %collective-permute-start.10 = (bf16[128,384]{1,0:T(8,128)(2,1)S(1)}, bf16[128,384]{1,0:T(8,128)(2,1)S(1)}, u32[]{:S(2)}, u32[]{:S(2)}) collective-permute-start(bf16[128,384]{1,0:T(8,128)(2,1)S(1)} %collective-permute-done.9), channel_id=1, source_target_pairs={{0,1},{1,2},{2,3},{3,4},{4,5},{5,6},{6,7},{7,8},{8,9},{9,10},{10,1... | collective-permute-start | bytes 294920 | tf_op jit(solution)/shard_map/ppermute | solution.py:46
  113.0 0.6 copy-start.14
  113.6 5.3 %collective-permute-start.11 = (bf16[128,384]{1,0:T(8,128)(2,1)S(1)}, bf16[128,384]{1,0:T(8,128)(2,1)S(1)}, u32[]{:S(2)}, u32[]{:S(2)}) collective-permute-start(bf16[128,384]{1,0:T(8,128)(2,1)S(1)} %collective-permute-done.10), channel_id=1, source_target_pairs={{0,1},{1,2},{2,3},{3,4},{4,5},{5,6},{6,7},{7,8},{8,9},{9,10},{10,1... | collective-permute-start | bytes 294920 | tf_op jit(solution)/shard_map/ppermute | solution.py:46
  118.9 0.6 copy-start.16
  119.5 5.3 %collective-permute-start.12 = (bf16[128,384]{1,0:T(8,128)(2,1)S(1)}, bf16[128,384]{1,0:T(8,128)(2,1)S(1)}, u32[]{:S(2)}, u32[]{:S(2)}) collective-permute-start(bf16[128,384]{1,0:T(8,128)(2,1)S(1)} %collective-permute-done.11), channel_id=1, source_target_pairs={{0,1},{1,2},{2,3},{3,4},{4,5},{5,6},{6,7},{7,8},{8,9},{9,10},{10,1... | collective-permute-start | bytes 294920 | tf_op jit(solution)/shard_map/ppermute | solution.py:46
  124.8 0.6 copy-start.18
  125.4 5.3 %collective-permute-start.13 = (bf16[128,384]{1,0:T(8,128)(2,1)S(1)}, bf16[128,384]{1,0:T(8,128)(2,1)S(1)}, u32[]{:S(2)}, u32[]{:S(2)}) collective-permute-start(bf16[128,384]{1,0:T(8,128)(2,1)S(1)} %collective-permute-done.12), channel_id=1, source_target_pairs={{0,1},{1,2},{2,3},{3,4},{4,5},{5,6},{6,7},{7,8},{8,9},{9,10},{10,1... | collective-permute-start | bytes 294920 | tf_op jit(solution)/shard_map/ppermute | solution.py:46
  130.7 0.6 copy-start.20
  130.7 5.4 %collective-permute-start.14 = (bf16[128,384]{1,0:T(8,128)(2,1)S(1)}, bf16[128,384]{1,0:T(8,128)(2,1)}, u32[]{:S(2)}, u32[]{:S(2)}) collective-permute-start(bf16[128,384]{1,0:T(8,128)(2,1)S(1)} %collective-permute-done.13), channel_id=1, source_target_pairs={{0,1},{1,2},{2,3},{3,4},{4,5},{5,6},{6,7},{7,8},{8,9},{9,10},{10,1... | collective-permute-start | bytes 294920 | tf_op jit(solution)/shard_map/ppermute | solution.py:46
  131.3 16.8 %copy-start.19 = (bf16[128,384]{1,0:T(8,128)(2,1)S(1)}, bf16[128,384]{1,0:T(8,128)(2,1)}, u32[]{:S(2)}) copy-start(bf16[128,384]{1,0:T(8,128)(2,1)} %copy-done.18) | copy-start | bytes 294916
  131.3 16.8 %copy-start.17 = (bf16[128,384]{1,0:T(8,128)(2,1)S(1)}, bf16[128,384]{1,0:T(8,128)(2,1)}, u32[]{:S(2)}) copy-start(bf16[128,384]{1,0:T(8,128)(2,1)} %copy-done.16) | copy-start | bytes 294916
  131.3 16.9 %copy-start.15 = (bf16[128,384]{1,0:T(8,128)(2,1)S(1)}, bf16[128,384]{1,0:T(8,128)(2,1)}, u32[]{:S(2)}) copy-start(bf16[128,384]{1,0:T(8,128)(2,1)} %copy-done.14) | copy-start | bytes 294916
  131.3 16.9 %copy-start.13 = (bf16[128,384]{1,0:T(8,128)(2,1)S(1)}, bf16[128,384]{1,0:T(8,128)(2,1)}, u32[]{:S(2)}) copy-start(bf16[128,384]{1,0:T(8,128)(2,1)} %copy-done.12) | copy-start | bytes 294916
  131.3 16.9 %copy-start.11 = (bf16[128,384]{1,0:T(8,128)(2,1)S(1)}, bf16[128,384]{1,0:T(8,128)(2,1)}, u32[]{:S(2)}) copy-start(bf16[128,384]{1,0:T(8,128)(2,1)} %copy-done.10) | copy-start | bytes 294916
  131.3 17.0 %copy-start.9 = (bf16[128,384]{1,0:T(8,128)(2,1)S(1)}, bf16[128,384]{1,0:T(8,128)(2,1)}, u32[]{:S(2)}) copy-start(bf16[128,384]{1,0:T(8,128)(2,1)} %copy-done.8) | copy-start | bytes 294916
  131.3 17.0 %copy-start.7 = (bf16[128,384]{1,0:T(8,128)(2,1)S(1)}, bf16[128,384]{1,0:T(8,128)(2,1)}, u32[]{:S(2)}) copy-start(bf16[128,384]{1,0:T(8,128)(2,1)} %copy-done.6) | copy-start | bytes 294916
  131.4 17.0 %copy-start.5 = (bf16[128,384]{1,0:T(8,128)(2,1)S(1)}, bf16[128,384]{1,0:T(8,128)(2,1)}, u32[]{:S(2)}) copy-start(bf16[128,384]{1,0:T(8,128)(2,1)} %copy-done.4) | copy-start | bytes 294916
  131.4 17.0 %copy-start.3 = (bf16[128,384]{1,0:T(8,128)(2,1)S(1)}, bf16[128,384]{1,0:T(8,128)(2,1)}, u32[]{:S(2)}) copy-start(bf16[128,384]{1,0:T(8,128)(2,1)} %copy-done.2) | copy-start | bytes 294916
  131.4 17.1 %copy-start.1 = (bf16[128,384]{1,0:T(8,128)(2,1)S(1)}, bf16[128,384]{1,0:T(8,128)(2,1)}, u32[]{:S(2)}) copy-start(bf16[128,384]{1,0:T(8,128)(2,1)} %copy-done) | copy-start | bytes 294916
  136.0 12.0 %copy-start.21 = (bf16[128,384]{1,0:T(8,128)(2,1)S(1)}, bf16[128,384]{1,0:T(8,128)(2,1)}, u32[]{:S(2)}) copy-start(bf16[128,384]{1,0:T(8,128)(2,1)} %copy-done.20) | copy-start | bytes 294916
Sparse Core Ops, SparseCore 0:
  9.8 128.6 all-gather.1
